TPU v7x, 32 devices: a whole 2x2x4 slice. The times are simulated.
32 devices in a mesh: tm: 16 (over z, x, core), doc: 2 (over y).
Axes of the slice: x: 2, y: 2, z: 4, core: 2. Of those that a mesh axis runs over, the one named last changes fastest.
Arguments:
- beta: float32 [16, 4096, 128], P('tm', 'doc'), may hold values from -6 to 260
- word_ids: int32 [16, 8, 128], P('tm', 'doc'), may hold values from 0 to 4095
- word_counts: int32 [16, 8, 128], P('tm', 'doc'), may hold values from 1 to 8
- block_slot: int32 [32], replicated, may hold values from 0 to 31, each once
- topic_prior: float32 [128], replicated, may hold values from 0.05 to 0.5
- drift_var: float32 [128], replicated, may hold values from 0.0005 to 0.05
- obs_precision: float32 [16, 128], replicated, may hold values from 0.01 to 4
Outputs:
- smoothed_means: float32 [16, 4096, 128], P('tm', 'doc')
- doc_topics: float32 [16, 8, 128], P('tm', 'doc')
Inputs may be any that keep to these rules, and one draw needn't show every extreme that they name: `block_slot`: each block has its own position.
All inputs are finite; a program needn't handle non-finite values.
Results may differ from a plain program's by a relative error of at most 0.0012.
The roundings to bfloat16 on the way count: a program that leaves them out, or rounds other values in their place, can miss the bound.
Values may be sent and summed in bfloat16 or wider, within the bound.
No kernel may reach another device: no remote copies, remote signals or barrier semaphores. Data moves between devices by JAX's collectives and lax.ppermute only.
A program may use at most 192 MiB of HBM per device.

v0:
```python
import jax
import jax.numpy as jnp
from jax import lax
from jax.sharding import PartitionSpec as P

K = 128
BLOCK = 128
EITERS = 4
init_variance = 4.0


def joined(value, axis, combine):
    everything = jax.tree.map(lambda part: lax.all_gather(part, axis), value)
    initial = jax.tree.map(lambda part: part[0], everything)

    def step(k, so_far):
        return combine(so_far, jax.tree.map(lambda part: part[k], everything))

    return lax.fori_loop(1, lax.axis_size(axis), step, initial)


def entering(part, axis, combine, identity, reverse):
    count = lax.axis_size(axis)
    place = lax.axis_index(axis)
    ahead = count - 1 - place if reverse else place
    gathered = jax.tree.map(lambda a: lax.all_gather(a, axis), part)
    state = jax.tree.map(lambda a, e: jnp.zeros_like(a) + jnp.asarray(e, a.dtype), part, identity)

    def one(step, state):
        source = count - 1 - step if reverse else step
        return combine(
            state, jax.tree.map(lambda a: lax.dynamic_index_in_dim(a, source, 0, False), gathered)
        )

    return lax.fori_loop(0, ahead, one, state)


def variance_tables(obs_precision, drift_var):

    def forward_step(prior_var, precision):
        denominator = 1.0 + prior_var * precision
        gain_now = prior_var * precision / denominator
        filt_var = prior_var / denominator
        return (filt_var + drift_var, (gain_now, filt_var))

    start_var = jnp.full(drift_var.shape, init_variance, dtype=jnp.float32)
    last_var, (gains, filt_vars) = lax.scan(forward_step, start_var, obs_precision)

    def backward_step(info_next, precision):
        merged = info_next + precision
        shrink = 1.0 / (1.0 + drift_var * merged)
        info_now = merged * shrink
        return (info_now, (shrink, info_now))

    zero_info = jnp.zeros(drift_var.shape, dtype=jnp.float32)
    last_info, (shrinks, infos) = lax.scan(
        backward_step, zero_info, obs_precision[1:], reverse=True
    )
    shrinks = jnp.concatenate([shrinks, jnp.ones_like(zero_info)[None]], axis=0)
    infos = jnp.concatenate([infos, zero_info[None]], axis=0)
    return (gains, filt_vars, shrinks, infos)


def e_step(looked, word_counts, topic_prior):
    counts_float = word_counts.astype(jnp.float32)
    doc_topics = topic_prior + jnp.sum(counts_float, axis=-1, keepdims=True) / K
    scores = looked.astype(jnp.float32)
    for sweep in range(EITERS):
        resp = jax.nn.softmax(lax.digamma(doc_topics)[..., None, :] + scores, axis=-1)
        doc_topics = topic_prior + jnp.sum(counts_float[..., None] * resp, axis=-2)
    weighted = (counts_float[..., None] * resp).astype(jnp.bfloat16)
    return (doc_topics, weighted)


def combine_normalizer(first_part, second_part):
    peak_value = jnp.maximum(first_part[0], second_part[0])
    summed = first_part[1] * jnp.exp(first_part[0] - peak_value) + second_part[1] * jnp.exp(
        second_part[0] - peak_value
    )
    return (peak_value, summed)


def compose_maps(earlier, later):
    return (later[0] * earlier[0], later[0] * earlier[1] + later[1])


def pick_year(table_all, year_index):
    return lax.dynamic_index_in_dim(table_all, year_index, 0, keepdims=False)


def body(beta, word_ids, word_counts, block_slot, topic_prior, drift_var, obs_precision):
    local_beta = beta[0]
    own_words = local_beta.shape[0]
    topics = local_beta.shape[1]
    local_peak = jnp.max(local_beta, axis=0)
    local_total = jnp.sum(jnp.exp(local_beta - local_peak), axis=0)
    peak_value, total_value = joined((local_peak, local_total), "doc", combine_normalizer)
    table = (local_beta - (peak_value + jnp.log(total_value))).astype(jnp.bfloat16)
    slot_ids = word_ids[0]
    doc_count = slot_ids.shape[0]
    slot_width = slot_ids.shape[1]
    block_count = block_slot.shape[0]
    block_of = slot_ids // BLOCK
    block_match = block_of[..., None] == lax.iota(jnp.int32, block_count)
    columns = jnp.sum(jnp.where(block_match, block_slot, 0), axis=-1) * BLOCK + slot_ids % BLOCK
    flat_columns = columns.reshape(-1)
    slot_total = flat_columns.shape[0]
    piece = lax.all_gather(table, "doc", axis=0, tiled=True)
    inside = (flat_columns >= 0) & (flat_columns < piece.shape[0])
    picked = jnp.take(piece, jnp.clip(flat_columns, 0, piece.shape[0] - 1), axis=0)
    looked = jnp.where(inside[:, None], picked, jnp.zeros_like(picked)).reshape(
        doc_count, slot_width, topics
    )
    doc_topics, weighted = e_step(looked, word_counts[0], topic_prior)
    flat_weighted = weighted.reshape(slot_total, topics)
    row_words = lax.iota(jnp.int32, own_words * lax.axis_size("doc"))
    marks = (row_words[:, None] == flat_columns[None, :]).astype(jnp.bfloat16)
    counts = lax.psum_scatter(
        jnp.dot(marks, flat_weighted, preferred_element_type=jnp.float32).astype(jnp.bfloat16),
        "doc",
        scatter_dimension=0,
        tiled=True,
    ).astype(jnp.float32)
    pseudo = local_beta + jnp.log1p(counts)
    gains, filt_vars, shrinks, infos = variance_tables(obs_precision, drift_var)
    year_index = lax.axis_index("tm")
    years_total = obs_precision.shape[0]
    gain_now = pick_year(gains, year_index)
    filt_now = pick_year(filt_vars, year_index)
    keep_part = 1.0 - gain_now
    push_part = gain_now * pseudo
    identity_map = (jnp.ones_like(keep_part), jnp.zeros_like(push_part))
    before = entering((keep_part, push_part), "tm", compose_maps, identity_map, False)
    filtered = keep_part * before[1] + push_part
    pull_now = jnp.where(year_index == years_total - 1, 0.0, filt_now / (filt_now + drift_var))
    own_term = (1.0 - pull_now) * filtered
    after = entering((pull_now, own_term), "tm", compose_maps, identity_map, True)
    smoothed = pull_now * after[1] + own_term
    return (smoothed[None], doc_topics[None])


def solution(mesh):
    in_specs = (
        P("tm", "doc", None),
        P("tm", "doc", None),
        P("tm", "doc", None),
        P(),
        P(),
        P(),
        P(),
    )
    out_specs = (P("tm", "doc", None), P("tm", "doc", None))
    return jax.shard_map(body, mesh=mesh, in_specs=in_specs, out_specs=out_specs, check_vma=False)
```

profile of v0, /device:TPU:0, one launch (start us, length us, event | category | flops | bytes accessed | tf_op | source)
XLA Modules:
  0.0 387.6 jit_solution(6193052944169842220)
XLA Ops:
  7.2 1.6 reduce_max.53
  10.3 5.2 %all-gather.8 = f32[2,1,128]{2,1,0:T(1,128)S(1)} all-gather(f32[1,1,128]{2,1,0:T(1,128)S(1)} %bitcast.211), channel_id=4, replica_groups=mesh['tm'=16,'doc'=2] {'doc'}, dimensions={0}, use_global_device_ids=true | all-gather | bytes 1536 | tf_op jit(solution)/shard_map/all_gather | solution.py:13
  15.5 4.2 %all-gather.7 = f32[2,1,128]{2,1,0:T(1,128)S(1)} all-gather(f32[1,1,128]{2,1,0:T(1,128)S(1)} %bitcast.210), channel_id=3, replica_groups=mesh['tm'=16,'doc'=2] {'doc'}, dimensions={0}, use_global_device_ids=true | all-gather | bytes 1536 | tf_op jit(solution)/shard_map/all_gather | solution.py:13
  19.8 2.1 fusion.6
  27.8 17.2 %all-gather.13.cloned.1.call-done = bf16[4096,128]{1,0:T(8,128)(2,1)} async-done(((bf16[2048,128]{1,0:T(8,128)(2,1)}), bf16[4096,128]{1,0:T(8,128)(2,1)}) %all-gather.13.cloned.1.call-update) | async-done | bytes 1048592 | tf_op jit(solution)/shard_map/all_gather | solution.py:108
  45.1 2.4 gather_fusion
  53.1 2.4 fusion.2
  55.6 12.5 %while.49 = (s32[]{:T(128)}, f32[128]{0:T(128)S(1)}, f32[16,128]{1,0:T(8,128)S(1)}, f32[16,128]{1,0:T(8,128)S(1)}, f32[16,128]{1,0:T(8,128)}, /*index=5*/f32[128]{0:T(128)S(1)}, s32[]{:T(128)}, s32[]{:T(128)}) while((s32[]{:T(128)}, f32[128]{0:T(128)S(1)}, f32[16,128]{1,0:T(8,128)S(1)}, f32[16,128]{1,0:T(8,128)S(1)}, ...), condition=%wide.region_1.0_spmd.clone, body=%wide.region_0.0_spmd.clone.sunk | while | flops 771 | bytes 5235 | solution.py:47
  68.1 7.9 %reduce-scatter.2.cloned.1.call-done = bf16[2048,128]{1,0:T(8,128)(2,1)} async-done(((bf16[4096,128]{1,0:T(8,128)(2,1)}), bf16[2048,128]{1,0:T(8,128)(2,1)}) %reduce-scatter.2.cloned.1.call-update) | async-done | bytes 524304 | tf_op jit(solution)/shard_map/reduce_scatter | solution.py:118
  76.0 2.4 fusion.7
  78.5 21.7 %all-gather.6 = f32[16,1,128]{2,1,0:T(1,128)S(1)} all-gather(f32[1,1,128]{2,1,0:T(1,128)S(1)} %get-tuple-element.251), channel_id=1, replica_groups=mesh['tm'=16,'doc'=2] {'tm'}, dimensions={0}, use_global_device_ids=true | all-gather | bytes 8704 | tf_op jit(solution)/shard_map/all_gather | solution.py:26
  100.3 105.0 %all-gather.15.cloned.1.call-done = f32[32768,128]{1,0:T(8,128)} async-done(((f32[2048,128]{1,0:T(8,128)}), f32[32768,128]{1,0:T(8,128)}) %all-gather.15.cloned.1.call-update) | async-done | bytes 16777232 | tf_op jit(solution)/shard_map/all_gather | solution.py:26
  207.6 40.6 %all-gather.5 = f32[16,1,128]{2,1,0:T(1,128)S(1)} all-gather(f32[1,1,128]{2,1,0:T(1,128)S(1)} %bitcast.209), channel_id=2, replica_groups=mesh['tm'=16,'doc'=2] {'tm'}, dimensions={0}, use_global_device_ids=true | all-gather | bytes 8704 | tf_op jit(solution)/shard_map/all_gather | solution.py:26
  249.2 106.2 %all-gather.17.cloned.1.call-done = f32[32768,128]{1,0:T(8,128)} async-done(((f32[2048,128]{1,0:T(8,128)}), f32[32768,128]{1,0:T(8,128)}) %all-gather.17.cloned.1.call-update) | async-done | bytes 16777232 | tf_op jit(solution)/shard_map/all_gather | solution.py:26
  355.5 24.4 %while.48 = (s32[]{:T(128)}, f32[2048,128]{1,0:T(8,128)S(1)}, s32[]{:T(128)}, f32[16,128]{1,0:T(8,128)S(1)}, f32[16,2048,128]{2,1,0:T(8,128)}, /*index=5*/s32[]{:T(128)}, s32[]{:T(128)}, s32[]{:T(128)}, s32[]{:T(128)}) while((s32[]{:T(128)}, f32[2048,128]{1,0:T(8,128)S(1)}, s32[]{:T(128)}, f32[16,128]{1,0:T(8,128)S(1)}, ...), condition=%wide.region_21.22_spmd, body=%wide.region_20.21_spmd.sunk | while | flops 524294 | bytes 3147419 | solution.py:35
  355.6 1.7 bitcast_add_fusion.8
  357.2 1.6 bitcast_add_fusion.8
  358.9 1.6 bitcast_add_fusion.8
  360.5 1.6 bitcast_add_fusion.8
  365.4 1.6 bitcast_add_fusion.8
  367.0 1.6 bitcast_add_fusion.8
  368.6 1.6 bitcast_add_fusion.8
  370.2 1.6 bitcast_add_fusion.8
  371.9 1.6 bitcast_add_fusion.8
  (130 shorter events, 39.5 us)
Async XLA Ops:
  7.2 68.9 %copy-start = (f32[1,2048,128]{2,1,0:T(8,128)S(1)}, f32[1,2048,128]{2,1,0:T(8,128)}, u32[]{:S(2)}) copy-start(f32[1,2048,128]{2,1,0:T(8,128)} %param.13) | copy-start | bytes 3145732
  7.2 48.4 %copy-start.3 = (f32[128]{0:T(128)S(1)}, f32[128]{0:T(128)}, u32[]{:S(2)}) copy-start(f32[128]{0:T(128)} %param.18) | copy-start | bytes 1540
  7.2 37.9 %all-gather.13.cloned.1.call-start = ((), (), s32[]{:S(2)}) async-start(), calls=%async_computation.1 | async-start | bytes 1572864 | tf_op jit(solution)/shard_map/all_gather | solution.py:108
  21.9 54.2 %reduce-scatter.2.cloned.1.call-start = ((), (), s32[]{:S(2)}) async-start(), calls=%async_computation.2 | async-start | bytes 1572864 | tf_op jit(solution)/shard_map/reduce_scatter | solution.py:118
  55.5 149.8 %all-gather.15.cloned.1.call-start = ((), (), s32[]{:S(2)}) async-start(), calls=%async_computation.3 | async-start | bytes 17825792 | tf_op jit(solution)/shard_map/all_gather | solution.py:26
  78.5 277.0 %all-gather.17.cloned.1.call-start = ((), (), s32[]{:S(2)}) async-start(), calls=%async_computation.4 | async-start | bytes 17825792 | tf_op jit(solution)/shard_map/all_gather | solution.py:26
  205.2 1.2 copy-start.2
  205.3 43.3 %copy-start.4 = (f32[128]{0:T(128)S(1)}, f32[128]{0:T(128)}, u32[]{:S(2)}) copy-start(f32[128]{0:T(128)} %param.17) | copy-start | bytes 1540
  355.4 24.5 %copy-start.1 = (f32[2048,128]{1,0:T(8,128)S(1)}, f32[2048,128]{1,0:T(8,128)}, u32[]{:S(2)}) copy-start(f32[2048,128]{1,0:T(8,128)} %add_multiply_fusion) | copy-start | bytes 3145732
Sparse Core Ops, SparseCore 0:
  22.0 23.0 all-gather.12
  55.6 20.3 reduce-scatter.1
  78.8 126.4 all-gather.14
  207.8 147.5 all-gather.16
where the time goes:
time: 389 us; the launch traced here: 388 us
  waiting for transfers between devices  236 us (61%)
  blocking collectives  71.7 us (18%)
  other arithmetic  57.4 us (15%)
  between operations  14 us (4%)
  local copies, waits for them, and re-layouts  4.73 us (1%)
    all_gather x2, waiting for transfers between devices, entering(): gathered = jax.tree.map(lambda a: lax.all_gather(a, axis), part)  211 us
    all_gather x2, blocking collectives, entering(): gathered = jax.tree.map(lambda a: lax.all_gather(a, axis), part)  62.3 us
    add x15, other arithmetic, compose_maps(): return (later[0] * earlier[0], later[0] * earlier[1] + later[1])  23.9 us
    all_gather x1, waiting for transfers between devices, body(): piece = lax.all_gather(table, 'doc', axis=0, tiled=True)  17.2 us
    add x16, other arithmetic, forward_step(): return (filt_var + drift_var, (gain_now, filt_var))  11.3 us
    all_gather x2, blocking collectives, joined(): everything = jax.tree.map(lambda part: lax.all_gather(part, axis), value)  9.41 us
    reduce_scatter x1, waiting for transfers between devices, body(): lax.psum_scatter(jnp.dot(marks, flat_weighted, preferred_element_type=jnp...  7.95 us
  transfers between devices with their start and end apart: 4, of which 4 were waited for; matrix products, arithmetic and copies ran while one was open for 5% of the time, Pallas kernels for 0%

commit v1 on v0

--- a/solution.py
+++ b/solution.py
@@ -105,7 +105,14 @@
     columns = jnp.sum(jnp.where(block_match, block_slot, 0), axis=-1) * BLOCK + slot_ids % BLOCK
     flat_columns = columns.reshape(-1)
     slot_total = flat_columns.shape[0]
-    piece = lax.all_gather(table, "doc", axis=0, tiled=True)
+    clean, current_value = (lax.axis_size("doc"), lax.axis_index("doc"))
+    piece, all_rows = (table, 1)
+    while all_rows < clean:
+        k_now = lax.ppermute(piece, "doc", [(tick, tick ^ all_rows) for tick in range(clean)])
+        g_now = jnp.concatenate([piece, k_now], axis=0)
+        small = jnp.concatenate([k_now, piece], axis=0)
+        piece = jnp.where(current_value & all_rows == 0, g_now, small)
+        all_rows = 2 * all_rows
     inside = (flat_columns >= 0) & (flat_columns < piece.shape[0])
     picked = jnp.take(piece, jnp.clip(flat_columns, 0, piece.shape[0] - 1), axis=0)
     looked = jnp.where(inside[:, None], picked, jnp.zeros_like(picked)).reshape(

time: 389 us -> 374 us (0.961)
  other arithmetic: 57.4 us -> 48.3 us
  waiting for transfers between devices: 236 us -> 230 us
    all_gather x1 -> x0, waiting for transfers between devices: 17.2 us -> none  [body(): piece = lax.all_gather(table, 'doc', axis=0, tiled=True)]
    ppermute x0 -> x1, waiting for transfers between devices: none -> 9.06 us  [body(): lax.ppermute(piece, 'doc', [(tick, tick ^ all_rows) for tick in range(cle...]
  transfers between devices with their start and end apart: 4 -> 4, of which waited for: 4 -> 4; matrix products, arithmetic and copies ran while one was open for 5% -> 4% of each run, Pallas kernels for 0% -> 0%
where the time goes in v1:
time: 374 us; the launch traced here: 373 us
  waiting for transfers between devices  230 us (61%)
  blocking collectives  71.7 us (19%)
  other arithmetic  48.3 us (13%)
  between operations  14.1 us (4%)
  local copies, waits for them, and re-layouts  3.75 us (1%)
    all_gather x2, waiting for transfers between devices, entering(): gathered = jax.tree.map(lambda a: lax.all_gather(a, axis), part)  211 us
    all_gather x2, blocking collectives, entering(): gathered = jax.tree.map(lambda a: lax.all_gather(a, axis), part)  62.3 us
    add x15, other arithmetic, compose_maps(): return (later[0] * earlier[0], later[0] * earlier[1] + later[1])  23.9 us
    add x16, other arithmetic, forward_step(): return (filt_var + drift_var, (gain_now, filt_var))  11.3 us
    reduce_scatter x1, waiting for transfers between devices, body(): lax.psum_scatter(jnp.dot(marks, flat_weighted, preferred_element_type=jnp...  9.44 us
    all_gather x2, blocking collectives, joined(): everything = jax.tree.map(lambda part: lax.all_gather(part, axis), value)  9.41 us
    ppermute x1, waiting for transfers between devices, body(): lax.ppermute(piece, 'doc', [(tick, tick ^ all_rows) for tick in range(cle...  9.06 us
  transfers between devices with their start and end apart: 4, of which 4 were waited for; matrix products, arithmetic and copies ran while one was open for 4% of the time, Pallas kernels for 0%

profile of v1, /device:TPU:0, one launch (start us, length us, event | category | flops | bytes accessed | tf_op | source)
XLA Modules:
  0.0 372.9 jit_solution(8513320098338110711)
XLA Ops:
  10.4 5.2 %all-gather.8 = f32[2,1,128]{2,1,0:T(1,128)S(1)} all-gather(f32[1,1,128]{2,1,0:T(1,128)S(1)} %bitcast.211), channel_id=4, replica_groups=mesh['tm'=16,'doc'=2] {'doc'}, dimensions={0}, use_global_device_ids=true | all-gather | bytes 1536 | tf_op jit(solution)/shard_map/all_gather | solution.py:13
  15.5 4.2 %all-gather.7 = f32[2,1,128]{2,1,0:T(1,128)S(1)} all-gather(f32[1,1,128]{2,1,0:T(1,128)S(1)} %bitcast.210), channel_id=3, replica_groups=mesh['tm'=16,'doc'=2] {'doc'}, dimensions={0}, use_global_device_ids=true | all-gather | bytes 1536 | tf_op jit(solution)/shard_map/all_gather | solution.py:13
  19.9 2.1 collective-permute-start
  22.5 9.1 %collective-permute-done = bf16[2048,128]{1,0:T(8,128)(2,1)S(1)} collective-permute-done((bf16[2048,128]{1,0:T(8,128)(2,1)S(1)}, bf16[2048,128]{1,0:T(8,128)(2,1)S(1)}, u32[]{:S(2)}, u32[]{:S(2)}) %collective-permute-start) | collective-permute-done | bytes 524320 | tf_op jit(solution)/shard_map/ppermute | solution.py:111
  36.8 2.4 fusion.2
  39.3 12.5 %while.49 = (s32[]{:T(128)}, f32[128]{0:T(128)S(1)}, f32[16,128]{1,0:T(8,128)S(1)}, f32[16,128]{1,0:T(8,128)S(1)}, f32[16,128]{1,0:T(8,128)}, /*index=5*/f32[128]{0:T(128)S(1)}, s32[]{:T(128)}, s32[]{:T(128)}) while((s32[]{:T(128)}, f32[128]{0:T(128)S(1)}, f32[16,128]{1,0:T(8,128)S(1)}, f32[16,128]{1,0:T(8,128)S(1)}, ...), condition=%wide.region_1.0_spmd.clone, body=%wide.region_0.0_spmd.clone.sunk | while | flops 771 | bytes 5235 | solution.py:47
  51.8 9.4 %reduce-scatter.2.cloned.1.call-done = bf16[2048,128]{1,0:T(8,128)(2,1)} async-done(((bf16[4096,128]{1,0:T(8,128)(2,1)}), bf16[2048,128]{1,0:T(8,128)(2,1)}) %reduce-scatter.2.cloned.1.call-update) | async-done | bytes 524304 | tf_op jit(solution)/shard_map/reduce_scatter | solution.py:125
  61.3 2.4 fusion.7
  63.8 21.7 %all-gather.6 = f32[16,1,128]{2,1,0:T(1,128)S(1)} all-gather(f32[1,1,128]{2,1,0:T(1,128)S(1)} %get-tuple-element.251), channel_id=1, replica_groups=mesh['tm'=16,'doc'=2] {'tm'}, dimensions={0}, use_global_device_ids=true | all-gather | bytes 8704 | tf_op jit(solution)/shard_map/all_gather | solution.py:26
  85.5 105.0 %all-gather.12.cloned.1.call-done = f32[32768,128]{1,0:T(8,128)} async-done(((f32[2048,128]{1,0:T(8,128)}), f32[32768,128]{1,0:T(8,128)}) %all-gather.12.cloned.1.call-update) | async-done | bytes 16777232 | tf_op jit(solution)/shard_map/all_gather | solution.py:26
  192.9 40.6 %all-gather.5 = f32[16,1,128]{2,1,0:T(1,128)S(1)} all-gather(f32[1,1,128]{2,1,0:T(1,128)S(1)} %bitcast.209), channel_id=2, replica_groups=mesh['tm'=16,'doc'=2] {'tm'}, dimensions={0}, use_global_device_ids=true | all-gather | bytes 8704 | tf_op jit(solution)/shard_map/all_gather | solution.py:26
  234.5 106.2 %all-gather.14.cloned.1.call-done = f32[32768,128]{1,0:T(8,128)} async-done(((f32[2048,128]{1,0:T(8,128)}), f32[32768,128]{1,0:T(8,128)}) %all-gather.14.cloned.1.call-update) | async-done | bytes 16777232 | tf_op jit(solution)/shard_map/all_gather | solution.py:26
  340.8 24.5 %while.48 = (s32[]{:T(128)}, f32[2048,128]{1,0:T(8,128)S(1)}, s32[]{:T(128)}, f32[16,128]{1,0:T(8,128)S(1)}, f32[16,2048,128]{2,1,0:T(8,128)}, /*index=5*/s32[]{:T(128)}, s32[]{:T(128)}, s32[]{:T(128)}, s32[]{:T(128)}) while((s32[]{:T(128)}, f32[2048,128]{1,0:T(8,128)S(1)}, s32[]{:T(128)}, f32[16,128]{1,0:T(8,128)S(1)}, ...), condition=%wide.region_21.22_spmd, body=%wide.region_20.21_spmd.sunk | while | flops 524294 | bytes 3147419 | solution.py:35
  340.8 1.7 bitcast_add_fusion.8
  342.6 1.6 bitcast_add_fusion.8
  344.2 1.6 bitcast_add_fusion.8
  345.8 1.6 bitcast_add_fusion.8
  350.7 1.6 bitcast_add_fusion.8
  352.3 1.6 bitcast_add_fusion.8
  353.9 1.6 bitcast_add_fusion.8
  355.5 1.6 bitcast_add_fusion.8
  357.2 1.6 bitcast_add_fusion.8
  360.4 1.6 bitcast_add_fusion.8
  362.0 1.6 bitcast_add_fusion.8
  (136 shorter events, 32.3 us)
Async XLA Ops:
  7.2 12.6 %copy-start = (f32[1,2048,128]{2,1,0:T(8,128)S(1)}, f32[1,2048,128]{2,1,0:T(8,128)}, u32[]{:S(2)}) copy-start(f32[1,2048,128]{2,1,0:T(8,128)} %param.13) | copy-start | bytes 3145732
  7.2 14.8 %copy-start.3 = (s32[1,4,128]{2,1,0:T(4,128)S(1)}, s32[1,4,128]{2,1,0:T(4,128)}, u32[]{:S(2)}) copy-start(s32[1,4,128]{2,1,0:T(4,128)} %param.14) | copy-start | bytes 6148
  7.2 14.8 %copy-start.7 = (s32[32]{0:T(128)S(1)}, s32[32]{0:T(128)}, u32[]{:S(2)}) copy-start(s32[32]{0:T(128)} %param.16) | copy-start | bytes 388
  7.2 15.0 %copy-start.6 = (s32[1,4,128]{2,1,0:T(4,128)S(1)}, s32[1,4,128]{2,1,0:T(4,128)}, u32[]{:S(2)}) copy-start(s32[1,4,128]{2,1,0:T(4,128)} %param.15) | copy-start | bytes 6148
  7.2 15.2 %copy-start.5 = (f32[128]{0:T(128)S(1)}, f32[128]{0:T(128)}, u32[]{:S(2)}) copy-start(f32[128]{0:T(128)} %param.17) | copy-start | bytes 1540
  7.2 54.1 %reduce-scatter.2.cloned.1.call-start = ((), (), s32[]{:S(2)}) async-start(), calls=%async_computation.1 | async-start | bytes 1572864 | tf_op jit(solution)/shard_map/reduce_scatter | solution.py:125
  19.9 11.7 %collective-permute-start = (bf16[2048,128]{1,0:T(8,128)(2,1)S(1)}, bf16[2048,128]{1,0:T(8,128)(2,1)S(1)}, u32[]{:S(2)}, u32[]{:S(2)}) collective-permute-start(bf16[2048,128]{1,0:T(8,128)(2,1)S(1)} %fusion.6), channel_id=1, source_target_pairs={{0,1},{1,0},{2,3},{3,2},{4,5},{5,4},{6,7},{7,6},{8,9},{9,8},{10,11... | collective-permute-start | bytes 1572872 | tf_op jit(solution)/shard_map/ppermute | solution.py:111
  36.8 2.5 copy-start.4
  39.3 151.2 %all-gather.12.cloned.1.call-start = ((), (), s32[]{:S(2)}) async-start(), calls=%async_computation.2 | async-start | bytes 17825792 | tf_op jit(solution)/shard_map/all_gather | solution.py:26
  63.7 277.0 %all-gather.14.cloned.1.call-start = ((), (), s32[]{:S(2)}) async-start(), calls=%async_computation.3 | async-start | bytes 17825792 | tf_op jit(solution)/shard_map/all_gather | solution.py:26
  190.6 1.2 copy-start.2
  340.8 24.5 %copy-start.1 = (f32[2048,128]{1,0:T(8,128)S(1)}, f32[2048,128]{1,0:T(8,128)}, u32[]{:S(2)}) copy-start(f32[2048,128]{1,0:T(8,128)} %add_multiply_fusion) | copy-start | bytes 3145732
Sparse Core Ops, SparseCore 0:
  39.4 21.8 reduce-scatter.1
  64.0 126.4 all-gather.11
  193.3 147.4 all-gather.13
